TPU v7x, 32 devices: a whole 2x2x4 slice. The times are simulated.
32 devices in a mesh: dp: 8 (over y, x, core), tensor: 4 (over z).
Axes of the slice: x: 2, y: 2, z: 4, core: 2. Of those that a mesh axis runs over, the one named last changes fastest.
Arguments:
- inputs: bfloat16 [4096, 2048], P('dp'), may hold values from -6 to 6
- active: int32 [4096], P('dp'), may hold values from 0 to 1, as said below
- block_table: int32 [16], replicated, may hold values from 0 to 15, as said below
- gain_one: bfloat16 [2048], replicated, may hold values from 0.099609375 to 1.8984375
- w_query: bfloat16 [2048, 2048], P(None, 'tensor'), may hold values from -0.125 to 0.125
- w_key: bfloat16 [2048, 1024], P(None, 'tensor'), may hold values from -0.125 to 0.125
- w_value: bfloat16 [2048, 1024], P(None, 'tensor'), may hold values from -0.125 to 0.125
- w_out: bfloat16 [2048, 2048], P('tensor'), may hold values from -4 to 4
- gain_two: bfloat16 [2048], replicated, may hold values from 0.099609375 to 1.8984375
- w_gate: bfloat16 [2048, 5632], P(None, 'tensor'), may hold values from -0.125 to 0.125
- w_up: bfloat16 [2048, 5632], P(None, 'tensor'), may hold values from -0.125 to 0.125
- w_down: bfloat16 [5632, 2048], P('tensor'), may hold values from -0.078125 to 0.078125
- cotangent: bfloat16 [4096, 2048], P('dp'), may hold values from -6 to 6
Outputs:
- output: bfloat16 [4096, 2048], P('dp')
- grad_input: float32 [4096, 2048], P('dp')
- grad_gain_one: float32 [2048], replicated
- grad_w_query: float32 [2048, 2048], P(None, 'tensor')
- grad_w_key: float32 [2048, 1024], P(None, 'tensor')
- grad_w_value: float32 [2048, 1024], P(None, 'tensor')
- grad_w_out: float32 [2048, 2048], P('tensor')
- grad_gain_two: float32 [2048], replicated
- grad_w_gate: float32 [2048, 5632], P(None, 'tensor')
- grad_w_up: float32 [2048, 5632], P(None, 'tensor')
- grad_w_down: float32 [5632, 2048], P('tensor')
Inputs may be any that keep to these rules, and one draw needn't show every extreme that they name: `active`: 0 or 1 for every token; the share of 1s differs from one causal block to another. `block_table`: each causal block appears once; entries 2i and 2i+1 sum to 15.
All inputs are finite; a program needn't handle non-finite values.
Results may differ from a plain program's by a relative error of at most 0.014.
Values may be sent and summed in bfloat16 or wider, within the bound.
No kernel may reach another device: no remote copies, remote signals or barrier semaphores. Data moves between devices by JAX's collectives and lax.ppermute only.
A program may use at most 256 MiB of HBM per device.

v0:
```python
import jax
import jax.numpy as jnp
from jax import lax
from jax.sharding import PartitionSpec as P

HEAD_DIM = 128
EPS = 1e-05
MASKED_SCORE = -1e30


def rms_norm(values, scales):
    return values * lax.rsqrt(jnp.mean(values * values, axis=-1, keepdims=True) + EPS) * scales


def rotate(values, cos_table, sin_table):
    middle = values.shape[-1] // 2
    leading = values[..., :middle]
    trailing = values[..., middle:]
    return jnp.concatenate(
        [leading * cos_table - trailing * sin_table, trailing * cos_table + leading * sin_table],
        axis=-1,
    )


def angles_of(positions, head_size):
    frequency = 10000.0 ** (-jnp.arange(0, head_size, 2, dtype=jnp.float32) / head_size)
    angles = positions.astype(jnp.float32)[:, None] * frequency[None, :]
    return (jnp.cos(angles)[:, None, :], jnp.sin(angles)[:, None, :])


def swiglu(gate_value, up_value):
    return jax.nn.silu(gate_value) * up_value


def left_trans(left, right):
    return lax.dot_general(
        left, right, (((0,), (0,)), ((), ())), preferred_element_type=jnp.float32
    )


def right_trans(left, right):
    return lax.dot_general(
        left, right, (((1,), (1,)), ((), ())), preferred_element_type=jnp.float32
    )


def partner_perm(axis_size, mask):
    return [(index, index ^ mask) for index in range(axis_size)]


def permute_sum(parts, dims, axis):
    size = lax.axis_size(axis)
    steps = size.bit_length() - 1
    assert 1 << steps == size
    me = lax.axis_index(axis)
    pieces = list(parts)
    for step in range(steps):
        bit = me >> step & 1
        keep, send = ([], [])
        for piece, dim in zip(pieces, dims):
            half = piece.shape[dim] // 2
            keep.append(lax.dynamic_slice_in_dim(piece, bit * half, half, axis=dim))
            send.append(
                lax.dynamic_slice_in_dim(piece, (1 - bit) * half, half, axis=dim).astype(
                    jnp.bfloat16
                )
            )
        got = lax.ppermute(send, axis, partner_perm(size, 1 << step))
        pieces = [mine + theirs.astype(jnp.float32) for mine, theirs in zip(keep, got)]
    pieces = [piece.astype(jnp.bfloat16) for piece in pieces]
    for step in reversed(range(steps)):
        first = me >> step & 1 == 0
        got = lax.ppermute(pieces, axis, partner_perm(size, 1 << step))
        pieces = [
            jnp.concatenate(
                [jnp.where(first, mine, theirs), jnp.where(first, theirs, mine)], axis=dim
            )
            for mine, theirs, dim in zip(pieces, got, dims)
        ]
    return [piece.astype(jnp.float32) for piece in pieces]


def permute_allsum(value, axis):
    size = lax.axis_size(axis)
    steps = size.bit_length() - 1
    for step in range(steps):
        value = value + lax.ppermute(value, axis, partner_perm(size, 1 << step))
    return value


def on_device(
    inputs,
    active,
    block_table,
    gain_one,
    w_query,
    w_key,
    w_value,
    w_out,
    gain_two,
    w_gate,
    w_up,
    w_down,
    cotangent,
):
    row_count = inputs.shape[0]
    local_heads = w_query.shape[1] // HEAD_DIM
    local_groups = w_key.shape[1] // HEAD_DIM
    group_size = local_heads // local_groups
    half_rows = row_count // 2
    length = row_count * lax.axis_size("dp")
    score_scale = HEAD_DIM ** (-0.5)
    key_pos = (
        block_table[:, None] * half_rows + jnp.arange(half_rows, dtype=jnp.int32)[None, :]
    ).reshape(length)
    row_start = lax.axis_index("dp") * row_count
    query_pos = lax.dynamic_slice_in_dim(key_pos, row_start, row_count)
    slot_ids = jnp.arange(length, dtype=jnp.int32)
    own_ids = row_start + jnp.arange(row_count, dtype=jnp.int32)
    cos_table, sin_table = angles_of(query_pos, HEAD_DIM)
    keep_rows = active.astype(jnp.float32)[:, None]
    source = inputs.astype(jnp.float32)
    normed_full, norm_one_back = jax.vjp(rms_norm, source, gain_one.astype(jnp.float32))
    normed = normed_full.astype(jnp.bfloat16)
    query_raw = jnp.dot(normed, w_query, preferred_element_type=jnp.float32).reshape(
        row_count, local_heads, HEAD_DIM
    )
    key_raw = jnp.dot(normed, w_key, preferred_element_type=jnp.float32).reshape(
        row_count, local_groups, HEAD_DIM
    )
    value_low = jnp.dot(normed, w_value, preferred_element_type=jnp.float32).astype(jnp.bfloat16)
    query_low = (
        rotate(query_raw, cos_table, sin_table)
        .reshape(row_count, local_heads * HEAD_DIM)
        .astype(jnp.bfloat16)
    )
    key_low = (
        rotate(key_raw, cos_table, sin_table)
        .reshape(row_count, local_groups * HEAD_DIM)
        .astype(jnp.bfloat16)
    )
    alive_low = active.astype(jnp.bfloat16)

    def allowed_of(alive_all):
        return (key_pos[None, :] <= query_pos[:, None]) & (
            (alive_all[None, :] > 0) | (slot_ids[None, :] == own_ids[:, None])
        )

    def head_scores(head_index, keys_all, allowed):
        query_part = query_low[:, head_index * HEAD_DIM : (head_index + 1) * HEAD_DIM]
        group_index = head_index // group_size
        key_part = keys_all[:, group_index * HEAD_DIM : (group_index + 1) * HEAD_DIM]
        raw_scores = right_trans(query_part, key_part) * score_scale
        return jnp.where(allowed, raw_scores, MASKED_SCORE)

    kv_width = local_groups * HEAD_DIM
    all_kv = lax.all_gather(jnp.concatenate([key_low, value_low], axis=1), "dp", axis=0, tiled=True)
    all_keys = all_kv[:, :kv_width]
    all_values = all_kv[:, kv_width:]
    all_alive = lax.all_gather(alive_low, "dp", axis=0, tiled=True)
    allowed_fwd = allowed_of(all_alive)
    mixed_parts = []
    lse_parts = []
    for head_index in range(local_heads):
        masked = head_scores(head_index, all_keys, allowed_fwd)
        row_max = jnp.max(masked, axis=1, keepdims=True)
        shifted = jnp.exp(masked - row_max)
        row_total = jnp.sum(shifted, axis=1, keepdims=True)
        probs_low = (shifted / row_total).astype(jnp.bfloat16)
        lse_parts.append(row_max + jnp.log(row_total))
        group_index = head_index // group_size
        value_part = all_values[:, group_index * HEAD_DIM : (group_index + 1) * HEAD_DIM]
        mixed_parts.append(jnp.dot(probs_low, value_part, preferred_element_type=jnp.float32))
    attended = jnp.concatenate(mixed_parts, axis=1).astype(jnp.bfloat16)
    (branch,) = permute_sum(
        [jnp.dot(attended, w_out, preferred_element_type=jnp.float32)], [0], "tensor"
    )
    middle = source + keep_rows * branch
    normed_two_full, norm_two_back = jax.vjp(rms_norm, middle, gain_two.astype(jnp.float32))
    normed_two = normed_two_full.astype(jnp.bfloat16)
    gate_value = jnp.dot(normed_two, w_gate, preferred_element_type=jnp.float32)
    up_value = jnp.dot(normed_two, w_up, preferred_element_type=jnp.float32)
    hidden_full, swiglu_back = jax.vjp(swiglu, gate_value, up_value)
    hidden = hidden_full.astype(jnp.bfloat16)
    (down_sum,) = permute_sum(
        [jnp.dot(hidden, w_down, preferred_element_type=jnp.float32)], [0], "tensor"
    )
    output = (middle + keep_rows * down_sum).astype(jnp.bfloat16)
    grad_out = cotangent.astype(jnp.float32)
    d_down = (keep_rows * grad_out).astype(jnp.bfloat16)
    grad_w_down = left_trans(hidden, d_down)
    d_hidden = right_trans(d_down, w_down)
    d_gate_full, d_up_full = swiglu_back(d_hidden)
    d_gate = d_gate_full.astype(jnp.bfloat16)
    d_up = d_up_full.astype(jnp.bfloat16)
    grad_w_gate = left_trans(normed_two, d_gate)
    grad_w_up = left_trans(normed_two, d_up)
    (d_normed_two,) = permute_sum(
        [right_trans(d_gate, w_gate) + right_trans(d_up, w_up)], [0], "tensor"
    )
    d_middle_norm, grad_gain_two = norm_two_back(d_normed_two)
    grad_middle = grad_out + d_middle_norm
    d_branch = (keep_rows * grad_middle).astype(jnp.bfloat16)
    grad_w_out = left_trans(attended, d_branch)
    d_attended = right_trans(d_branch, w_out).astype(jnp.bfloat16)
    back_keys, back_values = (all_keys, all_values)
    allowed_back = allowed_fwd
    d_query_parts = []
    d_key_parts = [
        jnp.zeros((length, HEAD_DIM), jnp.float32) for group_index in range(local_groups)
    ]
    d_value_parts = [
        jnp.zeros((length, HEAD_DIM), jnp.float32) for group_index in range(local_groups)
    ]
    for head_index in range(local_heads):
        group_index = head_index // group_size
        masked = head_scores(head_index, back_keys, allowed_back)
        probs = jnp.where(allowed_back, jnp.exp(masked - lse_parts[head_index]), 0.0)
        probs_low = probs.astype(jnp.bfloat16)
        d_out_part = d_attended[:, head_index * HEAD_DIM : (head_index + 1) * HEAD_DIM]
        key_part = back_keys[:, group_index * HEAD_DIM : (group_index + 1) * HEAD_DIM]
        value_part = back_values[:, group_index * HEAD_DIM : (group_index + 1) * HEAD_DIM]
        query_part = query_low[:, head_index * HEAD_DIM : (head_index + 1) * HEAD_DIM]
        d_probs = right_trans(d_out_part, value_part)
        row_delta = jnp.sum(probs * d_probs, axis=1, keepdims=True)
        d_scores = (probs * (d_probs - row_delta)).astype(jnp.bfloat16)
        d_query_parts.append(
            jnp.dot(d_scores, key_part, preferred_element_type=jnp.float32) * score_scale
        )
        d_key_parts[group_index] = (
            d_key_parts[group_index] + left_trans(d_scores, query_part) * score_scale
        )
        d_value_parts[group_index] = d_value_parts[group_index] + left_trans(probs_low, d_out_part)
    d_key_all = jnp.concatenate(d_key_parts, axis=1)
    d_value_all = jnp.concatenate(d_value_parts, axis=1)
    d_kv_own = lax.psum_scatter(
        jnp.concatenate([d_key_all, d_value_all], axis=1).astype(jnp.bfloat16),
        "dp",
        scatter_dimension=0,
        tiled=True,
    ).astype(jnp.float32)
    d_key_own = d_kv_own[:, :kv_width]
    d_value_own = d_kv_own[:, kv_width:]
    d_queries = jnp.concatenate(d_query_parts, axis=1).reshape(row_count, local_heads, HEAD_DIM)
    d_query_low = (
        rotate(d_queries, cos_table, -sin_table)
        .reshape(row_count, local_heads * HEAD_DIM)
        .astype(jnp.bfloat16)
    )
    d_key_low = (
        rotate(d_key_own.reshape(row_count, local_groups, HEAD_DIM), cos_table, -sin_table)
        .reshape(row_count, local_groups * HEAD_DIM)
        .astype(jnp.bfloat16)
    )
    d_value_low = d_value_own.astype(jnp.bfloat16)
    grad_w_query = left_trans(normed, d_query_low)
    grad_w_key = left_trans(normed, d_key_low)
    grad_w_value = left_trans(normed, d_value_low)
    d_normed_part = (
        right_trans(d_query_low, w_query)
        + right_trans(d_key_low, w_key)
        + right_trans(d_value_low, w_value)
    )
    (d_normed,) = permute_sum([d_normed_part], [0], "tensor")
    d_source_norm, grad_gain_one = norm_one_back(d_normed)
    grad_input = grad_middle + d_source_norm
    grad_gain_one = permute_allsum(grad_gain_one, "dp")
    grad_gain_two = permute_allsum(grad_gain_two, "dp")

    def dp_sum(grads):
        return [lax.psum(grad.astype(jnp.bfloat16), "dp").astype(jnp.float32) for grad in grads]

    grad_w_gate, grad_w_up, grad_w_down = dp_sum([grad_w_gate, grad_w_up, grad_w_down])
    grad_w_gate, grad_w_up, grad_w_down, grad_w_out = lax.optimization_barrier(
        (grad_w_gate, grad_w_up, grad_w_down, grad_w_out)
    )
    (grad_w_out,) = dp_sum([grad_w_out])
    grad_w_out, grad_w_query, grad_w_key, grad_w_value = lax.optimization_barrier(
        (grad_w_out, grad_w_query, grad_w_key, grad_w_value)
    )
    grad_w_query, grad_w_key, grad_w_value = dp_sum([grad_w_query, grad_w_key, grad_w_value])
    return (
        output,
        grad_input,
        grad_gain_one,
        grad_w_query,
        grad_w_key,
        grad_w_value,
        grad_w_out,
        grad_gain_two,
        grad_w_gate,
        grad_w_up,
        grad_w_down,
    )


def solution(mesh):
    placed = (
        P("dp", None),
        P("dp"),
        P(),
        P(),
        P(None, "tensor"),
        P(None, "tensor"),
        P(None, "tensor"),
        P("tensor", None),
        P(),
        P(None, "tensor"),
        P(None, "tensor"),
        P("tensor", None),
        P("dp", None),
    )
    return jax.shard_map(
        on_device,
        mesh=mesh,
        in_specs=placed,
        out_specs=(
            P("dp", None),
            P("dp", None),
            P(),
            P(None, "tensor"),
            P(None, "tensor"),
            P(None, "tensor"),
            P("tensor", None),
            P(),
            P(None, "tensor"),
            P(None, "tensor"),
            P("tensor", None),
        ),
        check_vma=False,
    )
```

profile of v0, /device:TPU:0, one launch (start us, length us, event | category | flops | bytes accessed | tf_op | source)
XLA Modules:
  0.0 967.2 jit_solution(9074915309664158548)
XLA Ops:
  18.5 10.9 %all-gather = bf16[8,1,512]{2,1,0:T(2,128)(2,1)S(1)} all-gather(bf16[1,1,512]{2,1,0:T(2,128)(2,1)S(1)} %reshape.237), channel_id=1, replica_groups=mesh['dp'=8,'tensor'=4] {'dp'}, dimensions={0}, use_global_device_ids=true | all-gather | bytes 9216 | tf_op jit(solution)/shard_map/all_gather | solution.py:160
  33.4 25.2 %all-gather.3.cloned.1.call-done = bf16[4096,512]{0,1:T(8,128)(2,1)} async-done(((bf16[512,512]{0,1:T(8,128)(2,1)}), bf16[4096,512]{0,1:T(8,128)(2,1)}) %all-gather.3.cloned.1.call-update) | async-done | bytes 4194320 | tf_op jit(solution)/shard_map/all_gather | solution.py:157
  78.8 5.5 fusion.113
  85.6 7.1 fusion.38
  103.9 23.9 %collective-permute-done = bf16[256,2048]{1,0:T(8,128)(2,1)} collective-permute-done((bf16[256,2048]{1,0:T(8,128)(2,1)S(1)}, bf16[256,2048]{1,0:T(8,128)(2,1)}, u32[]{:S(2)}, u32[]{:S(2)}) %collective-permute-start) | collective-permute-done | bytes 1048608 | tf_op jit(solution)/shard_map/ppermute | solution.py:68
  133.9 22.9 %collective-permute-done.1 = bf16[128,2048]{1,0:T(8,128)(2,1)S(1)} collective-permute-done((bf16[128,2048]{1,0:T(8,128)(2,1)S(1)}, bf16[128,2048]{1,0:T(8,128)(2,1)S(1)}, u32[]{:S(2)}, u32[]{:S(2)}) %collective-permute-start.1) | collective-permute-done | bytes 524320 | tf_op jit(solution)/shard_map/ppermute | solution.py:68
  159.0 24.4 %collective-permute-done.2 = bf16[128,2048]{1,0:T(8,128)(2,1)} collective-permute-done((bf16[128,2048]{1,0:T(8,128)(2,1)S(1)}, bf16[128,2048]{1,0:T(8,128)(2,1)}, u32[]{:S(2)}, u32[]{:S(2)}) %collective-permute-start.2) | collective-permute-done | bytes 524320 | tf_op jit(solution)/shard_map/ppermute | solution.py:73
  185.7 6.5 fusion.43
  192.3 17.3 %collective-permute-done.3 = bf16[256,2048]{1,0:T(8,128)(2,1)} collective-permute-done((bf16[256,2048]{1,0:T(8,128)(2,1)}, bf16[256,2048]{1,0:T(8,128)(2,1)}, u32[]{:S(2)}, u32[]{:S(2)}) %collective-permute-start.3) | collective-permute-done | bytes 1048608 | tf_op jit(solution)/shard_map/ppermute | solution.py:73
  216.9 6.0 multiply_convert_fusion.6
  230.4 5.4 fusion.115
  237.8 18.3 %collective-permute-done.8 = bf16[256,2048]{1,0:T(8,128)(2,1)S(1)} collective-permute-done((bf16[256,2048]{1,0:T(8,128)(2,1)S(1)}, bf16[256,2048]{1,0:T(8,128)(2,1)S(1)}, u32[]{:S(2)}, u32[]{:S(2)}) %collective-permute-start.8) | collective-permute-done | bytes 1048608 | tf_op jit(solution)/shard_map/ppermute | solution.py:68
  258.2 28.2 %collective-permute-done.4 = bf16[256,2048]{1,0:T(8,128)(2,1)S(1)} collective-permute-done((bf16[256,2048]{1,0:T(8,128)(2,1)S(1)}, bf16[256,2048]{1,0:T(8,128)(2,1)S(1)}, u32[]{:S(2)}, u32[]{:S(2)}) %collective-permute-start.4) | collective-permute-done | bytes 1048608 | tf_op jit(solution)/shard_map/ppermute | solution.py:68
  290.1 34.2 %collective-permute-done.5 = bf16[128,2048]{1,0:T(8,128)(2,1)S(1)} collective-permute-done((bf16[128,2048]{1,0:T(8,128)(2,1)S(1)}, bf16[128,2048]{1,0:T(8,128)(2,1)S(1)}, u32[]{:S(2)}, u32[]{:S(2)}) %collective-permute-start.5) | collective-permute-done | bytes 524320 | tf_op jit(solution)/shard_map/ppermute | solution.py:68
  324.5 22.3 %collective-permute-done.10 = bf16[128,2048]{1,0:T(8,128)(2,1)S(1)} collective-permute-done((bf16[128,2048]{1,0:T(8,128)(2,1)S(1)}, bf16[128,2048]{1,0:T(8,128)(2,1)S(1)}, u32[]{:S(2)}, u32[]{:S(2)}) %collective-permute-start.10) | collective-permute-done | bytes 524320 | tf_op jit(solution)/shard_map/ppermute | solution.py:73
  347.1 9.8 %collective-permute-done.6 = bf16[128,2048]{1,0:T(8,128)(2,1)S(1)} collective-permute-done((bf16[128,2048]{1,0:T(8,128)(2,1)S(1)}, bf16[128,2048]{1,0:T(8,128)(2,1)S(1)}, u32[]{:S(2)}, u32[]{:S(2)}) %collective-permute-start.6) | collective-permute-done | bytes 524320 | tf_op jit(solution)/shard_map/ppermute | solution.py:73
  357.2 22.2 %collective-permute-done.11 = bf16[256,2048]{1,0:T(8,128)(2,1)S(1)} collective-permute-done((bf16[256,2048]{1,0:T(8,128)(2,1)S(1)}, bf16[256,2048]{1,0:T(8,128)(2,1)S(1)}, u32[]{:S(2)}, u32[]{:S(2)}) %collective-permute-start.11) | collective-permute-done | bytes 1048608 | tf_op jit(solution)/shard_map/ppermute | solution.py:73
  383.7 18.0 %collective-permute-done.7 = bf16[256,2048]{1,0:T(8,128)(2,1)S(1)} collective-permute-done((bf16[256,2048]{1,0:T(8,128)(2,1)S(1)}, bf16[256,2048]{1,0:T(8,128)(2,1)S(1)}, u32[]{:S(2)}, u32[]{:S(2)}) %collective-permute-start.7) | collective-permute-done | bytes 1048608 | tf_op jit(solution)/shard_map/ppermute | solution.py:73
  402.3 6.1 convert_add_fusion.1
  441.3 20.8 %multiply_reduce_fusion.2 = (f32[512]{0:T(512)S(1)}, f32[512]{0:T(512)S(1)}, f32[512]{0:T(512)S(1)}, f32[512]{0:T(512)}, f32[512,4096]{1,0:T(8,128)}) fusion(f32[512,4096]{1,0:T(8,128)S(1)} %bitcast.53, f32[512]{0:T(512)S(1)} %copy-done.69, s32[512]{0:T(512)S(1)} %copy-done.63, pred[4096]{0:T(1024)(128)(4,1)S(1)} %bitcast.97, s32[512]{0:T(512)S(1)} %copy-done.59, ...), kind=kOutput, calls=%fused_computation.7 | convolution fusion | flops 578811904 | bytes 68329472 | tf_op jit(solution)/shard_map/dot_general | solution.py:42
  462.0 18.5 %multiply_convert_fusion.2 = (bf16[512,4096]{1,0:T(8,128)(2,1)}, bf16[512,4096]{1,0:T(8,128)(2,1)}, bf16[512,4096]{1,0:T(8,128)(2,1)}) fusion(f32[512,4096]{1,0:T(8,128)} %get-tuple-element.88, f32[512]{0:T(512)S(1)} %get-tuple-element.31, f32[512,4096]{1,0:T(8,128)S(1)} %bitcast.53, f32[512]{0:T(512)S(1)} %copy-done.69, s32[512]{0:T(512)S(1)} %copy-done.63, ...), kind=kLoop, calls=%fused_computation.6 | loop fusion | flops 39845888 | bytes 62951424 | tf_op jit(solution)/shard_map/convert_element_type | solution.py:226
  483.6 8.7 multiply_convert_fusion
  500.8 6.8 convolution_convert_fusion.2
  507.6 5.3 convolution_convert_fusion.1
  531.9 18.0 %reduce-scatter.2.cloned.1.call-done = bf16[512,512]{0,1:T(8,128)(2,1)} async-done(((bf16[4096,512]{0,1:T(8,128)(2,1)}), bf16[512,512]{0,1:T(8,128)(2,1)}) %reduce-scatter.2.cloned.1.call-update) | async-done | bytes 524304 | tf_op jit(solution)/shard_map/reduce_scatter | solution.py:236
  558.0 23.2 %collective-permute-done.12 = bf16[256,2048]{1,0:T(8,128)(2,1)S(1)} collective-permute-done((bf16[256,2048]{1,0:T(8,128)(2,1)S(1)}, bf16[256,2048]{1,0:T(8,128)(2,1)S(1)}, u32[]{:S(2)}, u32[]{:S(2)}) %collective-permute-start.12) | collective-permute-done | bytes 1048608 | tf_op jit(solution)/shard_map/ppermute | solution.py:68
  591.7 185.1 %all-reduce.10.cloned.1.call-done = (bf16[2048,1408]{1,0:T(8,128)(2,1)}, bf16[2048,1408]{1,0:T(8,128)(2,1)}, bf16[1408,2048]{1,0:T(8,128)(2,1)}) async-done(((bf16[2048,1408]{1,0:T(8,128)(2,1)}, bf16[2048,1408]{1,0:T(8,128)(2,1)}, bf16[1408,2048]{1,0:T(8,128)(2,1)}), (bf16[2048,1408]{1,0:T(8,128)(2,1)}, bf16[2048,1408]{1,0:T(8,128)(2,1)}, bf16[1408,2048]{1,0:T(8,128)(2,1)})) %all-reduce.10.cloned.1.call-update) | async-done | bytes 17301520 | tf_op jit(solution)/shard_map/psum | solution.py:271
  776.8 8.6 convert_element_type.279
  790.6 6.2 convert_element_type.283
  804.8 54.0 %all-reduce.6.cloned.1.call-done = bf16[512,2048]{1,0:T(8,128)(2,1)} async-done(((bf16[512,2048]{1,0:T(8,128)(2,1)}), bf16[512,2048]{1,0:T(8,128)(2,1)}) %all-reduce.6.cloned.1.call-update) | async-done | bytes 2097168 | tf_op jit(solution)/shard_map/psum | solution.py:271
  870.9 17.1 %collective-permute-done.15 = bf16[256,2048]{1,0:T(8,128)(2,1)S(1)} collective-permute-done((bf16[256,2048]{1,0:T(8,128)(2,1)S(1)}, bf16[256,2048]{1,0:T(8,128)(2,1)S(1)}, u32[]{:S(2)}, u32[]{:S(2)}) %collective-permute-start.15) | collective-permute-done | bytes 1048608 | tf_op jit(solution)/shard_map/ppermute | solution.py:73
  890.7 52.6 %all-reduce.8.cloned.1.call-done = (bf16[2048,512]{1,0:T(8,128)(2,1)}, bf16[2048,256]{1,0:T(8,128)(2,1)}, bf16[2048,256]{1,0:T(8,128)(2,1)}) async-done(((bf16[2048,512]{1,0:T(8,128)(2,1)}, bf16[2048,256]{1,0:T(8,128)(2,1)}, bf16[2048,256]{1,0:T(8,128)(2,1)}), (bf16[2048,512]{1,0:T(8,128)(2,1)}, bf16[2048,256]{1,0:T(8,128)(2,1)}, bf16[2048,256]{1,0:T(8,128)(2,1)})) %all-reduce.8.cloned.1.call-update) | async-done | bytes 4194320 | tf_op jit(solution)/shard_map/psum | solution.py:271
  (370 shorter events, 212.3 us)
Async XLA Ops:
  7.2 91.7 %copy-start = (bf16[512,2048]{1,0:T(8,128)(2,1)S(1)}, bf16[512,2048]{1,0:T(8,128)(2,1)}, u32[]{:S(2)}) copy-start(bf16[512,2048]{1,0:T(8,128)(2,1)} %param.20) | copy-start | bytes 6291460
  7.2 51.4 %all-gather.3.cloned.1.call-start = ((), (), s32[]{:S(2)}) async-start(), calls=%async_computation.1 | async-start | bytes 4718592 | tf_op jit(solution)/shard_map/all_gather | solution.py:157
  15.2 63.6 %copy-start.57 = (s32[512]{0:T(512)}, s32[512]{0:T(512)S(1)}, u32[]{:S(2)}) copy-start(s32[512]{0:T(512)S(1)} %get-tuple-element.42) | copy-start | bytes 6148
  18.4 531.5 %reduce-scatter.2.cloned.1.call-start = ((), (), s32[]{:S(2)}) async-start(), calls=%async_computation.2 | async-start | bytes 4718592 | tf_op jit(solution)/shard_map/reduce_scatter | solution.py:236
  102.3 25.5 %collective-permute-start = (bf16[256,2048]{1,0:T(8,128)(2,1)S(1)}, bf16[256,2048]{1,0:T(8,128)(2,1)}, u32[]{:S(2)}, u32[]{:S(2)}) collective-permute-start(bf16[256,2048]{1,0:T(8,128)(2,1)S(1)} %dynamic-slice_convert_fusion.3), channel_id=1, source_target_pairs={{0,1},{1,0},{2,3},{3,2},{4,5},{5,4},{6,7},{7,6},{8,9},{9,8},{10,11... | collective-permute-start | bytes 3145736 | tf_op jit(solution)/shard_map/ppermute | solution.py:68
  131.4 25.4 %collective-permute-start.1 = (bf16[128,2048]{1,0:T(8,128)(2,1)S(1)}, bf16[128,2048]{1,0:T(8,128)(2,1)S(1)}, u32[]{:S(2)}, u32[]{:S(2)}) collective-permute-start(bf16[128,2048]{1,0:T(8,128)(2,1)S(1)} %dynamic-slice_convert_fusion.7), channel_id=1, source_target_pairs={{0,2},{1,3},{2,0},{3,1},{4,6},{5,7},{6,4},{7,5},{8,10},{9,11},{10,... | collective-permute-start | bytes 1572872 | tf_op jit(solution)/shard_map/ppermute | solution.py:68
  158.2 25.2 %collective-permute-start.2 = (bf16[128,2048]{1,0:T(8,128)(2,1)S(1)}, bf16[128,2048]{1,0:T(8,128)(2,1)}, u32[]{:S(2)}, u32[]{:S(2)}) collective-permute-start(bf16[128,2048]{1,0:T(8,128)(2,1)S(1)} %add_convert_fusion.4), channel_id=1, source_target_pairs={{0,2},{1,3},{2,0},{3,1},{4,6},{5,7},{6,4},{7,5},{8,10},{9,11},{10,... | collective-permute-start | bytes 1572872 | tf_op jit(solution)/shard_map/ppermute | solution.py:73
  185.7 23.8 %collective-permute-start.3 = (bf16[256,2048]{1,0:T(8,128)(2,1)}, bf16[256,2048]{1,0:T(8,128)(2,1)}, u32[]{:S(2)}, u32[]{:S(2)}) collective-permute-start(bf16[256,2048]{1,0:T(8,128)(2,1)} %pad_maximum_fusion.3), channel_id=1, source_target_pairs={{0,1},{1,0},{2,3},{3,2},{4,5},{5,4},{6,7},{7,6},{8,9},{9,8},{10,11... | collective-permute-start | bytes 3145736 | tf_op jit(solution)/shard_map/ppermute | solution.py:73
  230.1 26.1 %collective-permute-start.8 = (bf16[256,2048]{1,0:T(8,128)(2,1)S(1)}, bf16[256,2048]{1,0:T(8,128)(2,1)S(1)}, u32[]{:S(2)}, u32[]{:S(2)}) collective-permute-start(bf16[256,2048]{1,0:T(8,128)(2,1)S(1)} %dynamic-slice_convert_fusion.1), channel_id=1, source_target_pairs={{0,1},{1,0},{2,3},{3,2},{4,5},{5,4},{6,7},{7,6},{8,9},{9,8},{10,11... | collective-permute-start | bytes 3145736 | tf_op jit(solution)/shard_map/ppermute | solution.py:68
  236.0 50.5 %collective-permute-start.4 = (bf16[256,2048]{1,0:T(8,128)(2,1)S(1)}, bf16[256,2048]{1,0:T(8,128)(2,1)S(1)}, u32[]{:S(2)}, u32[]{:S(2)}) collective-permute-start(bf16[256,2048]{1,0:T(8,128)(2,1)S(1)} %dynamic-slice_convert_fusion.2), channel_id=1, source_target_pairs={{0,1},{1,0},{2,3},{3,2},{4,5},{5,4},{6,7},{7,6},{8,9},{9,8},{10,11... | collective-permute-start | bytes 3145736 | tf_op jit(solution)/shard_map/ppermute | solution.py:68
  256.6 32.9 %collective-permute-start.9 = (bf16[128,2048]{1,0:T(8,128)(2,1)S(1)}, bf16[128,2048]{1,0:T(8,128)(2,1)S(1)}, u32[]{:S(2)}, u32[]{:S(2)}) collective-permute-start(bf16[128,2048]{1,0:T(8,128)(2,1)S(1)} %dynamic-slice_convert_fusion.5), channel_id=1, source_target_pairs={{0,2},{1,3},{2,0},{3,1},{4,6},{5,7},{6,4},{7,5},{8,10},{9,11},{10,... | collective-permute-start | bytes 1572872 | tf_op jit(solution)/shard_map/ppermute | solution.py:68
  286.9 37.4 %collective-permute-start.5 = (bf16[128,2048]{1,0:T(8,128)(2,1)S(1)}, bf16[128,2048]{1,0:T(8,128)(2,1)S(1)}, u32[]{:S(2)}, u32[]{:S(2)}) collective-permute-start(bf16[128,2048]{1,0:T(8,128)(2,1)S(1)} %dynamic-slice_convert_fusion.6), channel_id=1, source_target_pairs={{0,2},{1,3},{2,0},{3,1},{4,6},{5,7},{6,4},{7,5},{8,10},{9,11},{10,... | collective-permute-start | bytes 1572872 | tf_op jit(solution)/shard_map/ppermute | solution.py:68
  289.5 57.2 %collective-permute-start.10 = (bf16[128,2048]{1,0:T(8,128)(2,1)S(1)}, bf16[128,2048]{1,0:T(8,128)(2,1)S(1)}, u32[]{:S(2)}, u32[]{:S(2)}) collective-permute-start(bf16[128,2048]{1,0:T(8,128)(2,1)S(1)} %add_convert_fusion.2), channel_id=1, source_target_pairs={{0,2},{1,3},{2,0},{3,1},{4,6},{5,7},{6,4},{7,5},{8,10},{9,11},{10,... | collective-permute-start | bytes 1572872 | tf_op jit(solution)/shard_map/ppermute | solution.py:73
  324.4 32.4 %collective-permute-start.6 = (bf16[128,2048]{1,0:T(8,128)(2,1)S(1)}, bf16[128,2048]{1,0:T(8,128)(2,1)S(1)}, u32[]{:S(2)}, u32[]{:S(2)}) collective-permute-start(bf16[128,2048]{1,0:T(8,128)(2,1)S(1)} %add_convert_fusion.3), channel_id=1, source_target_pairs={{0,2},{1,3},{2,0},{3,1},{4,6},{5,7},{6,4},{7,5},{8,10},{9,11},{10,... | collective-permute-start | bytes 1572872 | tf_op jit(solution)/shard_map/ppermute | solution.py:73
  346.9 32.4 %collective-permute-start.11 = (bf16[256,2048]{1,0:T(8,128)(2,1)S(1)}, bf16[256,2048]{1,0:T(8,128)(2,1)S(1)}, u32[]{:S(2)}, u32[]{:S(2)}) collective-permute-start(bf16[256,2048]{1,0:T(8,128)(2,1)S(1)} %pad_maximum_fusion.5), channel_id=1, source_target_pairs={{0,1},{1,0},{2,3},{3,2},{4,5},{5,4},{6,7},{7,6},{8,9},{9,8},{10,11... | collective-permute-start | bytes 3145736 | tf_op jit(solution)/shard_map/ppermute | solution.py:73
  347.0 70.8 %copy-start.74 = (f32[512]{0:T(512)}, f32[512]{0:T(512)S(1)}, u32[]{:S(2)}) copy-start(f32[512]{0:T(512)S(1)} %get-tuple-element.89) | copy-start | bytes 6148
  347.1 67.1 %copy-start.70 = (f32[512]{0:T(512)}, f32[512]{0:T(512)S(1)}, u32[]{:S(2)}) copy-start(f32[512]{0:T(512)S(1)} %get-tuple-element.92) | copy-start | bytes 6148
  347.1 75.4 %copy-start.68 = (f32[512]{0:T(512)}, f32[512]{0:T(512)S(1)}, u32[]{:S(2)}) copy-start(f32[512]{0:T(512)S(1)} %get-tuple-element.91) | copy-start | bytes 6148
  357.1 44.7 %collective-permute-start.7 = (bf16[256,2048]{1,0:T(8,128)(2,1)S(1)}, bf16[256,2048]{1,0:T(8,128)(2,1)S(1)}, u32[]{:S(2)}, u32[]{:S(2)}) collective-permute-start(bf16[256,2048]{1,0:T(8,128)(2,1)S(1)} %pad_maximum_fusion.4), channel_id=1, source_target_pairs={{0,1},{1,0},{2,3},{3,2},{4,5},{5,4},{6,7},{7,6},{8,9},{9,8},{10,11... | collective-permute-start | bytes 3145736 | tf_op jit(solution)/shard_map/ppermute | solution.py:73
  499.2 277.6 %all-reduce.10.cloned.1.call-start = ((), (), s32[]{:S(2)}) async-start(), calls=%async_computation.5 | async-start | bytes 34603008 | tf_op jit(solution)/shard_map/psum | solution.py:271
  518.1 340.8 %all-reduce.6.cloned.1.call-start = ((), (), s32[]{:S(2)}) async-start(), calls=%async_computation.3 | async-start | bytes 4194304 | tf_op jit(solution)/shard_map/psum | solution.py:271
  556.5 24.8 %collective-permute-start.12 = (bf16[256,2048]{1,0:T(8,128)(2,1)S(1)}, bf16[256,2048]{1,0:T(8,128)(2,1)S(1)}, u32[]{:S(2)}, u32[]{:S(2)}) collective-permute-start(bf16[256,2048]{1,0:T(8,128)(2,1)S(1)} %dynamic-slice_convert_fusion), channel_id=1, source_target_pairs={{0,1},{1,0},{2,3},{3,2},{4,5},{5,4},{6,7},{7,6},{8,9},{9,8},{10,11... | collective-permute-start | bytes 3145736 | tf_op jit(solution)/shard_map/ppermute | solution.py:68
  583.7 213.1 %collective-permute-start.13 = (bf16[128,2048]{1,0:T(8,128)(2,1)}, bf16[128,2048]{1,0:T(8,128)(2,1)}, u32[]{:S(2)}, u32[]{:S(2)}) collective-permute-start(bf16[128,2048]{1,0:T(8,128)(2,1)} %dynamic-slice_convert_fusion.4), channel_id=1, source_target_pairs={{0,2},{1,3},{2,0},{3,1},{4,6},{5,7},{6,4},{7,5},{8,10},{9,11},{10,... | collective-permute-start | bytes 1572872 | tf_op jit(solution)/shard_map/ppermute | solution.py:68
  796.8 146.4 %all-reduce.8.cloned.1.call-start = ((), (), s32[]{:S(2)}) async-start(), calls=%async_computation.4 | async-start | bytes 8388608 | tf_op jit(solution)/shard_map/psum | solution.py:271
  798.4 64.6 %collective-permute-start.14 = (bf16[128,2048]{1,0:T(8,128)(2,1)S(1)}, bf16[128,2048]{1,0:T(8,128)(2,1)}, u32[]{:S(2)}, u32[]{:S(2)}) collective-permute-start(bf16[128,2048]{1,0:T(8,128)(2,1)S(1)} %add_convert_fusion.1), channel_id=1, source_target_pairs={{0,2},{1,3},{2,0},{3,1},{4,6},{5,7},{6,4},{7,5},{8,10},{9,11},{10,... | collective-permute-start | bytes 1572872 | tf_op jit(solution)/shard_map/ppermute | solution.py:73
  864.2 23.8 %collective-permute-start.15 = (bf16[256,2048]{1,0:T(8,128)(2,1)S(1)}, bf16[256,2048]{1,0:T(8,128)(2,1)S(1)}, u32[]{:S(2)}, u32[]{:S(2)}) collective-permute-start(bf16[256,2048]{1,0:T(8,128)(2,1)S(1)} %pad_maximum_fusion.7), channel_id=1, source_target_pairs={{0,1},{1,0},{2,3},{3,2},{4,5},{5,4},{6,7},{7,6},{8,9},{9,8},{10,11... | collective-permute-start | bytes 3145736 | tf_op jit(solution)/shard_map/ppermute | solution.py:73
  865.7 1.2 collective-permute-start.19
  866.9 3.7 collective-permute-start.20
  870.5 19.6 %collective-permute-start.21 = (f32[2048]{0:T(1024)S(1)}, f32[2048]{0:T(1024)S(1)}, u32[]{:S(2)}, u32[]{:S(2)}) collective-permute-start(f32[2048]{0:T(1024)S(1)} %add.262), channel_id=1, source_target_pairs={{0,16},{4,20},{8,24},{12,28},{16,0},{20,4},{24,8},{28,12},{1,17},{... | collective-permute-start | bytes 24584 | tf_op jit(solution)/shard_map/ppermute | solution.py:87
  890.0 60.6 %collective-permute-start.16 = (f32[2048]{0:T(1024)S(1)}, f32[2048]{0:T(1024)S(1)}, u32[]{:S(2)}, u32[]{:S(2)}) collective-permute-start(f32[2048]{0:T(1024)S(1)} %get-tuple-element.29), channel_id=1, source_target_pairs={{0,4},{4,0},{8,12},{12,8},{16,20},{20,16},{24,28},{28,24},{1,5},{5... | collective-permute-start | bytes 24584 | tf_op jit(solution)/shard_map/ppermute | solution.py:87
  950.6 3.7 collective-permute-start.17
  954.3 5.6 collective-permute-start.18
  (97 other events, 842.8 us)
Sparse Core Ops, SparseCore 0:
  18.5 40.0 all-gather.2
  499.3 50.5 reduce-scatter.1
  554.7 222.0 all-reduce.9
  797.0 61.8 all-reduce.5
  863.1 80.0 all-reduce.7
where the time goes:
time: 971 us; the launch traced here: 967 us
  waiting for transfers between devices  624 us (64%)
  matrix products  170 us (18%)
  other arithmetic  105 us (11%)
  starting transfers between devices  23.2 us (2%)
  local copies, waits for them, and re-layouts  18.1 us (2%)
  between operations  15.7 us (2%)
  blocking collectives  10.9 us (1%)
    psum x3, waiting for transfers between devices, dp_sum(): lax.psum(grad.astype(jnp.bfloat16), 'dp').astype(jnp.float32)  292 us
    ppermute x8, waiting for transfers between devices, permute_sum(): got = lax.ppermute(send, axis, partner_perm(size, 1 << step))  151 us
    ppermute x8, waiting for transfers between devices, permute_sum(): got = lax.ppermute(pieces, axis, partner_perm(size, 1 << step))  131 us
    dot_general x15, matrix products, right_trans(): lax.dot_general(left, right, (((1,), (1,)), ((), ())), preferred_element_...  71 us
    dot_general x15, matrix products, left_trans(): lax.dot_general(left, right, (((0,), (0,)), ((), ())), preferred_element_...  48.8 us
    convert_element_type x7, other arithmetic, dp_sum(): lax.psum(grad.astype(jnp.bfloat16), 'dp').astype(jnp.float32)  31.4 us
    convert_element_type x2, other arithmetic, on_device(): d_scores = (probs * (d_probs - row_delta)).astype(jnp.bfloat16)  27.2 us
    all_gather x1, waiting for transfers between devices, on_device(): lax.all_gather(jnp.concatenate([key_low, value_low], axis=1), 'dp', axis=...  25.2 us
  transfers between devices with their start and end apart: 27, of which 21 were waited for; matrix products, arithmetic and copies ran while one was open for 11% of the time, Pallas kernels for 0%

commit v1 on v0

--- a/solution.py
+++ b/solution.py
@@ -6,6 +6,23 @@
 HEAD_DIM = 128
 EPS = 1e-05
 MASKED_SCORE = -1e30
+
+
+def in_order(parts, dim):
+    parts = jnp.moveaxis(parts, 0, dim)
+    shape = parts.shape
+    return parts.reshape(*shape[:dim], shape[dim] * shape[dim + 1], *shape[dim + 2 :])
+
+
+def gather_around(x, axis, dim):
+    size = lax.axis_size(axis)
+    upward = [(i, (i + 1) % size) for i in range(size)]
+    pieces = [x]
+    while len(pieces) < size:
+        pieces.append(lax.ppermute(pieces[-1], axis, upward))
+    index = lax.axis_index(axis)
+    pieces = jnp.stack(pieces)[(index - jnp.arange(size)) % size]
+    return in_order(pieces, dim)
 
 
 def rms_norm(values, scales):
@@ -154,7 +171,7 @@
         return jnp.where(allowed, raw_scores, MASKED_SCORE)
 
     kv_width = local_groups * HEAD_DIM
-    all_kv = lax.all_gather(jnp.concatenate([key_low, value_low], axis=1), "dp", axis=0, tiled=True)
+    all_kv = gather_around(jnp.concatenate([key_low, value_low], axis=1), "dp", 0)
     all_keys = all_kv[:, :kv_width]
     all_values = all_kv[:, kv_width:]
     all_alive = lax.all_gather(alive_low, "dp", axis=0, tiled=True)

time: 971 us -> 1020 us (1.050)
  waiting for transfers between devices: 624 us -> 646 us
  local copies, waits for them, and re-layouts: 18.1 us -> 36.8 us
    ppermute x0 -> x7, waiting for transfers between devices: none -> 43.6 us  [gather_around(): pieces.append(lax.ppermute(pieces[-1], axis, upward))]
    all_gather x1 -> x0, waiting for transfers between devices: 25.2 us -> none  [on_device(): lax.all_gather(jnp.concatenate([key_low, value_low], axis=1), 'dp', axis=...]
    gather x0 -> x2, local copies, waits for them, and re-layouts: none -> 11.5 us  [gather_around(): pieces = jnp.stack(pieces)[(index - jnp.arange(size)) % size]]
    unnamed x207 -> x211, local copies, waits for them, and re-layouts: 15.5 us -> 22 us
  transfers between devices with their start and end apart: 27 -> 33, of which waited for: 21 -> 26; matrix products, arithmetic and copies ran while one was open for 11% -> 11% of each run, Pallas kernels for 0% -> 0%
where the time goes in v1:
time: 1020 us; the launch traced here: 1010 us
  waiting for transfers between devices  646 us (63%)
  matrix products  166 us (16%)
  other arithmetic  112 us (11%)
  local copies, waits for them, and re-layouts  36.8 us (4%)
  starting transfers between devices  23.8 us (2%)
  between operations  15.6 us (2%)
  blocking collectives  11.7 us (1%)
    psum x3, waiting for transfers between devices, dp_sum(): lax.psum(grad.astype(jnp.bfloat16), 'dp').astype(jnp.float32)  292 us
    ppermute x8, waiting for transfers between devices, permute_sum(): got = lax.ppermute(send, axis, partner_perm(size, 1 << step))  144 us
    ppermute x8, waiting for transfers between devices, permute_sum(): got = lax.ppermute(pieces, axis, partner_perm(size, 1 << step))  132 us
    dot_general x15, matrix products, right_trans(): lax.dot_general(left, right, (((1,), (1,)), ((), ())), preferred_element_...  66.5 us
    dot_general x15, matrix products, left_trans(): lax.dot_general(left, right, (((0,), (0,)), ((), ())), preferred_element_...  54.1 us
    ppermute x7, waiting for transfers between devices, gather_around(): pieces.append(lax.ppermute(pieces[-1], axis, upward))  43.6 us
    convert_element_type x7, other arithmetic, dp_sum(): lax.psum(grad.astype(jnp.bfloat16), 'dp').astype(jnp.float32)  31.4 us
    reduce_scatter x1, waiting for transfers between devices, on_device(): lax.psum_scatter(jnp.concatenate([d_key_all, d_value_all], axis=1).astype...  27.8 us
  transfers between devices with their start and end apart: 33, of which 26 were waited for; matrix products, arithmetic and copies ran while one was open for 11% of the time, Pallas kernels for 0%

profile of v1, /device:TPU:0, one launch (start us, length us, event | category | flops | bytes accessed | tf_op | source)
XLA Modules:
  0.0 1012.6 jit_solution(16356995346346231810)
XLA Ops:
  16.4 9.7 collective-permute-done
  26.1 9.5 collective-permute-done.1
  36.4 11.7 %all-gather = bf16[8,1,512]{2,1,0:T(2,128)(2,1)S(1)} all-gather(bf16[1,1,512]{2,1,0:T(2,128)(2,1)S(1)} %reshape.298), channel_id=1, replica_groups=mesh['dp'=8,'tensor'=4] {'dp'}, dimensions={0}, use_global_device_ids=true | all-gather | bytes 9216 | tf_op jit(solution)/shard_map/all_gather | solution.py:177
  60.2 7.5 collective-permute-done.4
  70.2 7.2 collective-permute-done.5
  92.8 6.4 copy.25
  99.2 7.8 fusion.112
  118.6 7.8 fusion.5
  150.1 18.9 %collective-permute-done.7 = bf16[256,2048]{1,0:T(8,128)(2,1)} collective-permute-done((bf16[256,2048]{1,0:T(8,128)(2,1)S(1)}, bf16[256,2048]{1,0:T(8,128)(2,1)}, u32[]{:S(2)}, u32[]{:S(2)}) %collective-permute-start.7) | collective-permute-done | bytes 1048608 | tf_op jit(solution)/shard_map/ppermute | solution.py:85
  175.4 18.2 %collective-permute-done.8 = bf16[128,2048]{1,0:T(8,128)(2,1)S(1)} collective-permute-done((bf16[128,2048]{1,0:T(8,128)(2,1)S(1)}, bf16[128,2048]{1,0:T(8,128)(2,1)S(1)}, u32[]{:S(2)}, u32[]{:S(2)}) %collective-permute-start.8) | collective-permute-done | bytes 524320 | tf_op jit(solution)/shard_map/ppermute | solution.py:85
  195.7 24.5 %collective-permute-done.9 = bf16[128,2048]{1,0:T(8,128)(2,1)} collective-permute-done((bf16[128,2048]{1,0:T(8,128)(2,1)S(1)}, bf16[128,2048]{1,0:T(8,128)(2,1)}, u32[]{:S(2)}, u32[]{:S(2)}) %collective-permute-start.9) | collective-permute-done | bytes 524320 | tf_op jit(solution)/shard_map/ppermute | solution.py:90
  222.6 6.5 fusion.43
  229.1 18.0 %collective-permute-done.10 = bf16[256,2048]{1,0:T(8,128)(2,1)} collective-permute-done((bf16[256,2048]{1,0:T(8,128)(2,1)}, bf16[256,2048]{1,0:T(8,128)(2,1)}, u32[]{:S(2)}, u32[]{:S(2)}) %collective-permute-start.10) | collective-permute-done | bytes 1048608 | tf_op jit(solution)/shard_map/ppermute | solution.py:90
  275.3 26.0 %collective-permute-done.15 = bf16[256,2048]{1,0:T(8,128)(2,1)S(1)} collective-permute-done((bf16[256,2048]{1,0:T(8,128)(2,1)S(1)}, bf16[256,2048]{1,0:T(8,128)(2,1)S(1)}, u32[]{:S(2)}, u32[]{:S(2)}) %collective-permute-start.15) | collective-permute-done | bytes 1048608 | tf_op jit(solution)/shard_map/ppermute | solution.py:85
  301.8 25.0 %collective-permute-done.11 = bf16[256,2048]{1,0:T(8,128)(2,1)S(1)} collective-permute-done((bf16[256,2048]{1,0:T(8,128)(2,1)S(1)}, bf16[256,2048]{1,0:T(8,128)(2,1)S(1)}, u32[]{:S(2)}, u32[]{:S(2)}) %collective-permute-start.11) | collective-permute-done | bytes 1048608 | tf_op jit(solution)/shard_map/ppermute | solution.py:85
  330.4 32.6 %collective-permute-done.12 = bf16[128,2048]{1,0:T(8,128)(2,1)S(1)} collective-permute-done((bf16[128,2048]{1,0:T(8,128)(2,1)S(1)}, bf16[128,2048]{1,0:T(8,128)(2,1)S(1)}, u32[]{:S(2)}, u32[]{:S(2)}) %collective-permute-start.12) | collective-permute-done | bytes 524320 | tf_op jit(solution)/shard_map/ppermute | solution.py:85
  363.2 22.3 %collective-permute-done.17 = bf16[128,2048]{1,0:T(8,128)(2,1)S(1)} collective-permute-done((bf16[128,2048]{1,0:T(8,128)(2,1)S(1)}, bf16[128,2048]{1,0:T(8,128)(2,1)S(1)}, u32[]{:S(2)}, u32[]{:S(2)}) %collective-permute-start.17) | collective-permute-done | bytes 524320 | tf_op jit(solution)/shard_map/ppermute | solution.py:90
  385.8 10.0 collective-permute-done.13
  396.1 22.2 %collective-permute-done.18 = bf16[256,2048]{1,0:T(8,128)(2,1)S(1)} collective-permute-done((bf16[256,2048]{1,0:T(8,128)(2,1)S(1)}, bf16[256,2048]{1,0:T(8,128)(2,1)S(1)}, u32[]{:S(2)}, u32[]{:S(2)}) %collective-permute-start.18) | collective-permute-done | bytes 1048608 | tf_op jit(solution)/shard_map/ppermute | solution.py:90
  422.7 18.0 %collective-permute-done.14 = bf16[256,2048]{1,0:T(8,128)(2,1)S(1)} collective-permute-done((bf16[256,2048]{1,0:T(8,128)(2,1)S(1)}, bf16[256,2048]{1,0:T(8,128)(2,1)S(1)}, u32[]{:S(2)}, u32[]{:S(2)}) %collective-permute-start.14) | collective-permute-done | bytes 1048608 | tf_op jit(solution)/shard_map/ppermute | solution.py:90
  468.0 7.5 fusion.13
  480.2 19.7 %multiply_reduce_fusion.2 = (f32[512]{0:T(512)S(1)}, f32[512]{0:T(512)S(1)}, f32[512]{0:T(512)S(1)}, f32[512]{0:T(512)}, f32[512,4096]{1,0:T(8,128)}) fusion(f32[512,4096]{1,0:T(8,128)} %copy-done.7, f32[512]{0:T(512)} %copy-done.72, s32[512]{0:T(512)S(1)} %copy-done.65, pred[4096]{0:T(1024)(128)(4,1)S(1)} %bitcast.129, s32[512]{0:T(512)S(1)} %copy-done.62, ...), kind=kOutput, calls=%fused_computation.8 | convolution fusion | flops 578811904 | bytes 68329472 | tf_op jit(solution)/shard_map/dot_general | solution.py:59
  499.9 18.1 %multiply_convert_fusion.2 = (bf16[512,4096]{1,0:T(8,128)(2,1)}, bf16[512,4096]{1,0:T(8,128)(2,1)}, bf16[512,4096]{1,0:T(8,128)(2,1)}) fusion(f32[512,4096]{1,0:T(8,128)} %get-tuple-element.88, f32[512]{0:T(512)S(1)} %get-tuple-element.31, f32[512,4096]{1,0:T(8,128)} %copy-done.7, f32[512]{0:T(512)S(1)} %copy-done.73, s32[512]{0:T(512)S(1)} %copy-done.65, ...), kind=kLoop, calls=%fused_computation.7 | loop fusion | flops 39845888 | bytes 62951424 | tf_op jit(solution)/shard_map/convert_element_type | solution.py:243
  521.0 9.2 multiply_convert_fusion
  538.6 6.8 convolution_convert_fusion.2
  567.5 27.8 %reduce-scatter.2.cloned.1.call-done = bf16[512,512]{0,1:T(8,128)(2,1)} async-done(((bf16[4096,512]{0,1:T(8,128)(2,1)}), bf16[512,512]{0,1:T(8,128)(2,1)}) %reduce-scatter.2.cloned.1.call-update) | async-done | bytes 524304 | tf_op jit(solution)/shard_map/reduce_scatter | solution.py:253
  603.4 23.3 %collective-permute-done.19 = bf16[256,2048]{1,0:T(8,128)(2,1)S(1)} collective-permute-done((bf16[256,2048]{1,0:T(8,128)(2,1)S(1)}, bf16[256,2048]{1,0:T(8,128)(2,1)S(1)}, u32[]{:S(2)}, u32[]{:S(2)}) %collective-permute-start.19) | collective-permute-done | bytes 1048608 | tf_op jit(solution)/shard_map/ppermute | solution.py:85
  637.1 185.1 %all-reduce.10.cloned.1.call-done = (bf16[2048,1408]{1,0:T(8,128)(2,1)}, bf16[2048,1408]{1,0:T(8,128)(2,1)}, bf16[1408,2048]{1,0:T(8,128)(2,1)}) async-done(((bf16[2048,1408]{1,0:T(8,128)(2,1)}, bf16[2048,1408]{1,0:T(8,128)(2,1)}, bf16[1408,2048]{1,0:T(8,128)(2,1)}), (bf16[2048,1408]{1,0:T(8,128)(2,1)}, bf16[2048,1408]{1,0:T(8,128)(2,1)}, bf16[1408,2048]{1,0:T(8,128)(2,1)})) %all-reduce.10.cloned.1.call-update) | async-done | bytes 17301520 | tf_op jit(solution)/shard_map/psum | solution.py:288
  822.2 8.6 convert_element_type.279
  850.2 54.0 %all-reduce.6.cloned.1.call-done = bf16[512,2048]{1,0:T(8,128)(2,1)} async-done(((bf16[512,2048]{1,0:T(8,128)(2,1)}), bf16[512,2048]{1,0:T(8,128)(2,1)}) %all-reduce.6.cloned.1.call-update) | async-done | bytes 2097168 | tf_op jit(solution)/shard_map/psum | solution.py:288
  916.3 17.1 %collective-permute-done.22 = bf16[256,2048]{1,0:T(8,128)(2,1)S(1)} collective-permute-done((bf16[256,2048]{1,0:T(8,128)(2,1)S(1)}, bf16[256,2048]{1,0:T(8,128)(2,1)S(1)}, u32[]{:S(2)}, u32[]{:S(2)}) %collective-permute-start.22) | collective-permute-done | bytes 1048608 | tf_op jit(solution)/shard_map/ppermute | solution.py:90
  936.0 52.6 %all-reduce.8.cloned.1.call-done = (bf16[2048,512]{1,0:T(8,128)(2,1)}, bf16[2048,256]{1,0:T(8,128)(2,1)}, bf16[2048,256]{1,0:T(8,128)(2,1)}) async-done(((bf16[2048,512]{1,0:T(8,128)(2,1)}, bf16[2048,256]{1,0:T(8,128)(2,1)}, bf16[2048,256]{1,0:T(8,128)(2,1)}), (bf16[2048,512]{1,0:T(8,128)(2,1)}, bf16[2048,256]{1,0:T(8,128)(2,1)}, bf16[2048,256]{1,0:T(8,128)(2,1)})) %all-reduce.8.cloned.1.call-update) | async-done | bytes 4194320 | tf_op jit(solution)/shard_map/psum | solution.py:288
  (391 shorter events, 257.3 us)
Async XLA Ops:
  7.2 588.1 %reduce-scatter.2.cloned.1.call-start = ((), (), s32[]{:S(2)}) async-start(), calls=%async_computation.1 | async-start | bytes 4718592 | tf_op jit(solution)/shard_map/reduce_scatter | solution.py:253
  15.8 10.3 %collective-permute-start = (bf16[512,512]{0,1:T(8,128)(2,1)S(1)}, bf16[512,512]{0,1:T(8,128)(2,1)S(1)}, u32[]{:S(2)}, u32[]{:S(2)}) collective-permute-start(bf16[512,512]{0,1:T(8,128)(2,1)S(1)} %pad_maximum_fusion.9), channel_id=1, source_target_pairs={{0,4},{4,8},{8,12},{12,16},{16,20},{20,24},{24,28},{28,0},{1,5},{5... | collective-permute-start | bytes 1572872 | tf_op jit(solution)/shard_map/ppermute | solution.py:22
  26.1 9.5 collective-permute-start.1
  36.4 11.8 %collective-permute-start.2 = (bf16[512,512]{0,1:T(8,128)(2,1)S(1)}, bf16[512,512]{0,1:T(8,128)(2,1)S(1)}, u32[]{:S(2)}, u32[]{:S(2)}) collective-permute-start(bf16[512,512]{0,1:T(8,128)(2,1)S(1)} %collective-permute-done.1), channel_id=1, source_target_pairs={{0,4},{4,8},{8,12},{12,16},{16,20},{20,24},{24,28},{28,0},{1,5},{5... | collective-permute-start | bytes 1572872 | tf_op jit(solution)/shard_map/ppermute | solution.py:22
  48.2 9.7 collective-permute-start.3
  57.9 9.8 collective-permute-start.4
  67.7 9.7 collective-permute-start.5
  77.4 9.5 collective-permute-start.6
  147.6 21.4 %collective-permute-start.7 = (bf16[256,2048]{1,0:T(8,128)(2,1)S(1)}, bf16[256,2048]{1,0:T(8,128)(2,1)}, u32[]{:S(2)}, u32[]{:S(2)}) collective-permute-start(bf16[256,2048]{1,0:T(8,128)(2,1)S(1)} %dynamic-slice_convert_fusion.3), channel_id=1, source_target_pairs={{0,1},{1,0},{2,3},{3,2},{4,5},{5,4},{6,7},{7,6},{8,9},{9,8},{10,11... | collective-permute-start | bytes 3145736 | tf_op jit(solution)/shard_map/ppermute | solution.py:85
  172.6 21.0 %collective-permute-start.8 = (bf16[128,2048]{1,0:T(8,128)(2,1)S(1)}, bf16[128,2048]{1,0:T(8,128)(2,1)S(1)}, u32[]{:S(2)}, u32[]{:S(2)}) collective-permute-start(bf16[128,2048]{1,0:T(8,128)(2,1)S(1)} %dynamic-slice_convert_fusion.7), channel_id=1, source_target_pairs={{0,2},{1,3},{2,0},{3,1},{4,6},{5,7},{6,4},{7,5},{8,10},{9,11},{10,... | collective-permute-start | bytes 1572872 | tf_op jit(solution)/shard_map/ppermute | solution.py:85
  194.9 25.3 %collective-permute-start.9 = (bf16[128,2048]{1,0:T(8,128)(2,1)S(1)}, bf16[128,2048]{1,0:T(8,128)(2,1)}, u32[]{:S(2)}, u32[]{:S(2)}) collective-permute-start(bf16[128,2048]{1,0:T(8,128)(2,1)S(1)} %add_convert_fusion.4), channel_id=1, source_target_pairs={{0,2},{1,3},{2,0},{3,1},{4,6},{5,7},{6,4},{7,5},{8,10},{9,11},{10,... | collective-permute-start | bytes 1572872 | tf_op jit(solution)/shard_map/ppermute | solution.py:90
  222.6 24.6 %collective-permute-start.10 = (bf16[256,2048]{1,0:T(8,128)(2,1)}, bf16[256,2048]{1,0:T(8,128)(2,1)}, u32[]{:S(2)}, u32[]{:S(2)}) collective-permute-start(bf16[256,2048]{1,0:T(8,128)(2,1)} %pad_maximum_fusion.3), channel_id=1, source_target_pairs={{0,1},{1,0},{2,3},{3,2},{4,5},{5,4},{6,7},{7,6},{8,9},{9,8},{10,11... | collective-permute-start | bytes 3145736 | tf_op jit(solution)/shard_map/ppermute | solution.py:90
  269.6 31.7 %collective-permute-start.15 = (bf16[256,2048]{1,0:T(8,128)(2,1)S(1)}, bf16[256,2048]{1,0:T(8,128)(2,1)S(1)}, u32[]{:S(2)}, u32[]{:S(2)}) collective-permute-start(bf16[256,2048]{1,0:T(8,128)(2,1)S(1)} %dynamic-slice_convert_fusion.1), channel_id=1, source_target_pairs={{0,1},{1,0},{2,3},{3,2},{4,5},{5,4},{6,7},{7,6},{8,9},{9,8},{10,11... | collective-permute-start | bytes 3145736 | tf_op jit(solution)/shard_map/ppermute | solution.py:85
  273.5 53.3 %collective-permute-start.11 = (bf16[256,2048]{1,0:T(8,128)(2,1)S(1)}, bf16[256,2048]{1,0:T(8,128)(2,1)S(1)}, u32[]{:S(2)}, u32[]{:S(2)}) collective-permute-start(bf16[256,2048]{1,0:T(8,128)(2,1)S(1)} %dynamic-slice_convert_fusion.2), channel_id=1, source_target_pairs={{0,1},{1,0},{2,3},{3,2},{4,5},{5,4},{6,7},{7,6},{8,9},{9,8},{10,11... | collective-permute-start | bytes 3145736 | tf_op jit(solution)/shard_map/ppermute | solution.py:85
  301.7 26.4 %collective-permute-start.16 = (bf16[128,2048]{1,0:T(8,128)(2,1)S(1)}, bf16[128,2048]{1,0:T(8,128)(2,1)S(1)}, u32[]{:S(2)}, u32[]{:S(2)}) collective-permute-start(bf16[128,2048]{1,0:T(8,128)(2,1)S(1)} %dynamic-slice_convert_fusion.5), channel_id=1, source_target_pairs={{0,2},{1,3},{2,0},{3,1},{4,6},{5,7},{6,4},{7,5},{8,10},{9,11},{10,... | collective-permute-start | bytes 1572872 | tf_op jit(solution)/shard_map/ppermute | solution.py:85
  327.2 35.8 %collective-permute-start.12 = (bf16[128,2048]{1,0:T(8,128)(2,1)S(1)}, bf16[128,2048]{1,0:T(8,128)(2,1)S(1)}, u32[]{:S(2)}, u32[]{:S(2)}) collective-permute-start(bf16[128,2048]{1,0:T(8,128)(2,1)S(1)} %dynamic-slice_convert_fusion.6), channel_id=1, source_target_pairs={{0,2},{1,3},{2,0},{3,1},{4,6},{5,7},{6,4},{7,5},{8,10},{9,11},{10,... | collective-permute-start | bytes 1572872 | tf_op jit(solution)/shard_map/ppermute | solution.py:85
  328.3 57.2 %collective-permute-start.17 = (bf16[128,2048]{1,0:T(8,128)(2,1)S(1)}, bf16[128,2048]{1,0:T(8,128)(2,1)S(1)}, u32[]{:S(2)}, u32[]{:S(2)}) collective-permute-start(bf16[128,2048]{1,0:T(8,128)(2,1)S(1)} %add_convert_fusion.2), channel_id=1, source_target_pairs={{0,2},{1,3},{2,0},{3,1},{4,6},{5,7},{6,4},{7,5},{8,10},{9,11},{10,... | collective-permute-start | bytes 1572872 | tf_op jit(solution)/shard_map/ppermute | solution.py:90
  363.2 32.7 %collective-permute-start.13 = (bf16[128,2048]{1,0:T(8,128)(2,1)S(1)}, bf16[128,2048]{1,0:T(8,128)(2,1)S(1)}, u32[]{:S(2)}, u32[]{:S(2)}) collective-permute-start(bf16[128,2048]{1,0:T(8,128)(2,1)S(1)} %add_convert_fusion.3), channel_id=1, source_target_pairs={{0,2},{1,3},{2,0},{3,1},{4,6},{5,7},{6,4},{7,5},{8,10},{9,11},{10,... | collective-permute-start | bytes 1572872 | tf_op jit(solution)/shard_map/ppermute | solution.py:90
  385.7 32.6 %collective-permute-start.18 = (bf16[256,2048]{1,0:T(8,128)(2,1)S(1)}, bf16[256,2048]{1,0:T(8,128)(2,1)S(1)}, u32[]{:S(2)}, u32[]{:S(2)}) collective-permute-start(bf16[256,2048]{1,0:T(8,128)(2,1)S(1)} %pad_maximum_fusion.5), channel_id=1, source_target_pairs={{0,1},{1,0},{2,3},{3,2},{4,5},{5,4},{6,7},{7,6},{8,9},{9,8},{10,11... | collective-permute-start | bytes 3145736 | tf_op jit(solution)/shard_map/ppermute | solution.py:90
  396.0 44.7 %collective-permute-start.14 = (bf16[256,2048]{1,0:T(8,128)(2,1)S(1)}, bf16[256,2048]{1,0:T(8,128)(2,1)S(1)}, u32[]{:S(2)}, u32[]{:S(2)}) collective-permute-start(bf16[256,2048]{1,0:T(8,128)(2,1)S(1)} %pad_maximum_fusion.4), channel_id=1, source_target_pairs={{0,1},{1,0},{2,3},{3,2},{4,5},{5,4},{6,7},{7,6},{8,9},{9,8},{10,11... | collective-permute-start | bytes 3145736 | tf_op jit(solution)/shard_map/ppermute | solution.py:90
  537.1 285.1 %all-reduce.10.cloned.1.call-start = ((), (), s32[]{:S(2)}) async-start(), calls=%async_computation.4 | async-start | bytes 34603008 | tf_op jit(solution)/shard_map/psum | solution.py:288
  555.9 348.2 %all-reduce.6.cloned.1.call-start = ((), (), s32[]{:S(2)}) async-start(), calls=%async_computation.2 | async-start | bytes 4194304 | tf_op jit(solution)/shard_map/psum | solution.py:288
  601.8 24.8 %collective-permute-start.19 = (bf16[256,2048]{1,0:T(8,128)(2,1)S(1)}, bf16[256,2048]{1,0:T(8,128)(2,1)S(1)}, u32[]{:S(2)}, u32[]{:S(2)}) collective-permute-start(bf16[256,2048]{1,0:T(8,128)(2,1)S(1)} %dynamic-slice_convert_fusion), channel_id=1, source_target_pairs={{0,1},{1,0},{2,3},{3,2},{4,5},{5,4},{6,7},{7,6},{8,9},{9,8},{10,11... | collective-permute-start | bytes 3145736 | tf_op jit(solution)/shard_map/ppermute | solution.py:85
  629.1 213.1 %collective-permute-start.20 = (bf16[128,2048]{1,0:T(8,128)(2,1)}, bf16[128,2048]{1,0:T(8,128)(2,1)}, u32[]{:S(2)}, u32[]{:S(2)}) collective-permute-start(bf16[128,2048]{1,0:T(8,128)(2,1)} %dynamic-slice_convert_fusion.4), channel_id=1, source_target_pairs={{0,2},{1,3},{2,0},{3,1},{4,6},{5,7},{6,4},{7,5},{8,10},{9,11},{10,... | collective-permute-start | bytes 1572872 | tf_op jit(solution)/shard_map/ppermute | solution.py:85
  842.2 146.4 %all-reduce.8.cloned.1.call-start = ((), (), s32[]{:S(2)}) async-start(), calls=%async_computation.3 | async-start | bytes 8388608 | tf_op jit(solution)/shard_map/psum | solution.py:288
  843.8 64.6 %collective-permute-start.21 = (bf16[128,2048]{1,0:T(8,128)(2,1)S(1)}, bf16[128,2048]{1,0:T(8,128)(2,1)}, u32[]{:S(2)}, u32[]{:S(2)}) collective-permute-start(bf16[128,2048]{1,0:T(8,128)(2,1)S(1)} %add_convert_fusion.1), channel_id=1, source_target_pairs={{0,2},{1,3},{2,0},{3,1},{4,6},{5,7},{6,4},{7,5},{8,10},{9,11},{10,... | collective-permute-start | bytes 1572872 | tf_op jit(solution)/shard_map/ppermute | solution.py:90
  909.6 23.8 %collective-permute-start.22 = (bf16[256,2048]{1,0:T(8,128)(2,1)S(1)}, bf16[256,2048]{1,0:T(8,128)(2,1)S(1)}, u32[]{:S(2)}, u32[]{:S(2)}) collective-permute-start(bf16[256,2048]{1,0:T(8,128)(2,1)S(1)} %pad_maximum_fusion.7), channel_id=1, source_target_pairs={{0,1},{1,0},{2,3},{3,2},{4,5},{5,4},{6,7},{7,6},{8,9},{9,8},{10,11... | collective-permute-start | bytes 3145736 | tf_op jit(solution)/shard_map/ppermute | solution.py:90
  912.2 3.7 collective-permute-start.27
  915.9 19.6 %collective-permute-start.28 = (f32[2048]{0:T(1024)S(1)}, f32[2048]{0:T(1024)S(1)}, u32[]{:S(2)}, u32[]{:S(2)}) collective-permute-start(f32[2048]{0:T(1024)S(1)} %add.287), channel_id=1, source_target_pairs={{0,16},{4,20},{8,24},{12,28},{16,0},{20,4},{24,8},{28,12},{1,17},{... | collective-permute-start | bytes 24584 | tf_op jit(solution)/shard_map/ppermute | solution.py:104
  935.3 60.6 %collective-permute-start.23 = (f32[2048]{0:T(1024)S(1)}, f32[2048]{0:T(1024)S(1)}, u32[]{:S(2)}, u32[]{:S(2)}) collective-permute-start(f32[2048]{0:T(1024)S(1)} %get-tuple-element.29), channel_id=1, source_target_pairs={{0,4},{4,0},{8,12},{12,8},{16,20},{20,16},{24,28},{28,24},{1,5},{5... | collective-permute-start | bytes 24584 | tf_op jit(solution)/shard_map/ppermute | solution.py:104
  995.9 3.7 collective-permute-start.24
  999.6 5.6 collective-permute-start.25
  (102 other events, 1708.6 us)
Sparse Core Ops, SparseCore 0:
  537.2 58.0 reduce-scatter.1
  600.1 222.0 all-reduce.9
  842.3 61.8 all-reduce.5
  908.5 80.0 all-reduce.7
